TPU v7x, 512 devices: a whole 4x8x8 slice. The times are simulated.
512 devices in a mesh: ctx: 32 (over y, x), fsdp: 16 (over z, core).
Axes of the slice: x: 4, y: 8, z: 8, core: 2. Of those that a mesh axis runs over, the one named last changes fastest.
Arguments:
- tokens: bfloat16 [131072, 4096], P(('ctx', 'fsdp')), may hold values from -48 to 48
- query_weight: bfloat16 [4096, 512], P('fsdp'), may hold values from -0.09375 to 0.09375
- key_weight: bfloat16 [4096, 128], P('fsdp'), may hold values from -0.09375 to 0.09375
- value_weight: bfloat16 [4096, 128], P('fsdp'), may hold values from -0.09375 to 0.09375
- chosen: int32 [256, 2], replicated, may hold values from 0 to 253, as said below
Outputs:
- attended: bfloat16 [131072, 512], P(('ctx', 'fsdp'))
Inputs may be any that keep to these rules, and one draw needn't show every extreme that they name: `chosen`: for query block q >= 3 both entries are distinct and below q - 1; block 2 names block 0 twice; blocks 0 and 1 name 0 twice, which selects nothing. The last block always selects block 253.
All inputs are finite; a program needn't handle non-finite values.
Results may differ from a plain program's by a relative error of at most 0.0065.
The roundings to bfloat16 on the way count: a program that leaves them out, or rounds other values in their place, can miss the bound.
Values may be sent and summed in bfloat16 or wider, within the bound.
No kernel may reach another device: no remote copies, remote signals or barrier semaphores. Data moves between devices by JAX's collectives and lax.ppermute only.
A program may use at most 64 MiB of HBM per device.

v0:
```python
import jax
import jax.numpy as jnp
from jax import lax
from jax.sharding import PartitionSpec as P

QH = 4


def from_behind(array, axis, by):
    peers = lax.axis_size(axis)
    pairs = [(i, i + by) for i in range(peers) if 0 <= i + by < peers]
    return lax.ppermute(array, axis, pairs)


def project_rows(tokens, pieces):
    return tuple(
        (
            jnp.dot(tokens, weight_piece, preferred_element_type=jnp.float32)
            for weight_piece in pieces
        )
    )


def per_device(tokens, query_weight, key_weight, value_weight, chosen):
    token_rows = tokens.shape[0]
    head_width = key_weight.shape[1]
    pair_width = 2 * head_width
    lane_count = lax.axis_size("fsdp")
    lane_index = lax.axis_index("fsdp")
    group_index = lax.axis_index("ctx")
    blocks_group = lane_count // 2
    my_block = group_index * blocks_group + lane_index // 2
    global_index = group_index * lane_count + lane_index
    projected = project_rows(
        tokens,
        (
            lax.all_gather(query_weight, "fsdp", axis=0, tiled=True),
            lax.all_gather(key_weight, "fsdp", axis=0, tiled=True),
            lax.all_gather(value_weight, "fsdp", axis=0, tiled=True),
        ),
    )
    queries = projected[0].astype(jnp.bfloat16).reshape(token_rows, QH, head_width)
    key_value = jnp.concatenate(
        [projected[1].astype(jnp.bfloat16), projected[2].astype(jnp.bfloat16)], axis=1
    )
    before_pair = from_behind(key_value, ("ctx", "fsdp"), 1)
    own_block = jnp.concatenate([before_pair, key_value], axis=0)
    candidates = lax.all_gather(key_value, "ctx", axis=0, tiled=True).reshape(
        -1, token_rows, pair_width
    )
    wanted = jnp.repeat(
        lax.dynamic_slice_in_dim(chosen, group_index * blocks_group, blocks_group, 0), 2, axis=0
    )
    dest_block = group_index * blocks_group + jnp.arange(lane_count, dtype=jnp.int32) // 2
    live_first = wanted[:, 0] < dest_block - 1
    live_second = (wanted[:, 1] < dest_block - 1) & (wanted[:, 1] != wanted[:, 0])
    mine = lax.dynamic_index_in_dim(chosen, my_block, 0, keepdims=False)
    sending = jnp.stack([live_first, live_second], axis=1) & (
        wanted % blocks_group == lane_index // 2
    )
    outgoing = jnp.take(candidates, (wanted // blocks_group).reshape(-1), axis=0)
    outgoing = outgoing.reshape(lane_count, 2, token_rows, pair_width)
    outgoing = jnp.where(sending[:, :, None, None], outgoing, jnp.zeros_like(outgoing))
    incoming = lax.all_to_all(outgoing, "fsdp", split_axis=0, concat_axis=0, tiled=True)

    def assemble(which):
        place = mine[which] % blocks_group * 2
        column_slot = incoming[:, which]
        return jnp.concatenate(
            [
                lax.dynamic_index_in_dim(column_slot, place, 0, keepdims=False),
                lax.dynamic_index_in_dim(column_slot, place + 1, 0, keepdims=False),
            ],
            axis=0,
        )

    block_first = assemble(0)
    block_second = assemble(1)
    key_rows = jnp.concatenate(
        [own_block[:, :head_width], block_first[:, :head_width], block_second[:, :head_width]],
        axis=0,
    )
    value_rows = jnp.concatenate(
        [own_block[:, head_width:], block_first[:, head_width:], block_second[:, head_width:]],
        axis=0,
    )
    scores = jnp.einsum(
        "qhd,kd->hqk", queries, key_rows, preferred_element_type=jnp.float32
    ) * head_width ** (-0.5)
    window_rows = own_block.shape[0]
    pick_rows = block_first.shape[0]
    row_index = jnp.arange(token_rows, dtype=jnp.int32)
    column = jnp.arange(window_rows, dtype=jnp.int32)
    causal = (column[None, :] <= row_index[:, None] + token_rows) & (
        (column[None, :] >= token_rows) | (global_index > 0)
    )
    first_ok = mine[0] < my_block - 1
    second_ok = (mine[1] < my_block - 1) & (mine[1] != mine[0])
    visible = jnp.concatenate(
        [
            causal,
            jnp.broadcast_to(first_ok, (token_rows, pick_rows)),
            jnp.broadcast_to(second_ok, (token_rows, pick_rows)),
        ],
        axis=1,
    )
    scores = jnp.where(visible[None], scores, -jnp.inf)
    highest = jnp.max(scores, axis=2, keepdims=True)
    probs = jnp.exp(scores - highest)
    denominator = jnp.sum(probs, axis=2, keepdims=True)
    mixed = (
        jnp.einsum(
            "hqk,kd->hqd",
            probs.astype(jnp.bfloat16),
            value_rows,
            preferred_element_type=jnp.float32,
        )
        / denominator
    )
    return jnp.transpose(mixed, (1, 0, 2)).reshape(token_rows, -1).astype(jnp.bfloat16)


def solution(mesh):
    return jax.shard_map(
        per_device,
        mesh=mesh,
        in_specs=(P(("ctx", "fsdp"), None), P("fsdp", None), P("fsdp", None), P("fsdp", None), P()),
        out_specs=P(("ctx", "fsdp"), None),
        check_vma=False,
    )
```

profile of v0, /device:TPU:6, one launch (start us, length us, event | category | flops | bytes accessed | tf_op | source)
XLA Modules:
  0.0 340.2 jit_solution(2382489390191044968)
XLA Ops:
  6.5 0.0 copy-start
  6.5 0.0 copy-start.2
  6.5 0.0 all-gather.7.cloned.1.call-start
  6.5 0.7 all-gather.7.cloned.1.call-update
  7.3 0.0 all-gather.5.cloned.1.call-start
  7.3 0.7 all-gather.5.cloned.1.call-update
  8.0 0.0 all-gather.9.cloned.1.call-start
  8.1 48.0 %all-gather.7.cloned.1.call-done = bf16[4096,128]{1,0:T(8,128)(2,1)} async-done(((bf16[256,128]{1,0:T(8,128)(2,1)}), bf16[4096,128]{1,0:T(8,128)(2,1)}) %all-gather.7.cloned.1.call-update) | async-done | bytes 1048592 | tf_op jit(solution)/shard_map/all_gather | solution.py:39
  56.1 0.0 copy-done
  56.1 2.1 convolution_convert_fusion.1
  58.1 40.2 %all-gather.5.cloned.1.call-done = bf16[4096,128]{1,0:T(8,128)(2,1)} async-done(((bf16[256,128]{1,0:T(8,128)(2,1)}), bf16[4096,128]{1,0:T(8,128)(2,1)}) %all-gather.5.cloned.1.call-update) | async-done | bytes 1048592 | tf_op jit(solution)/shard_map/all_gather | solution.py:38
  98.3 2.1 convolution_convert_fusion.2
  100.3 0.7 pad_maximum_fusion.2
  101.0 0.0 all-gather.9.cloned.1.call-update
  101.0 0.0 all-gather.11.cloned.1.call-start
  101.1 0.5 all-gather.11.cloned.1.call-update
  101.6 0.0 copy-done.2
  101.6 0.1 constant_dynamic-slice_fusion
  101.7 0.1 copy.15
  101.8 0.1 reshape.211
  101.9 0.1 copy.27
  102.0 0.1 copy.17
  102.1 0.1 copy.18
  102.2 86.4 %all-gather.9.cloned.1.call-done = bf16[8192,256]{0,1:T(8,128)(2,1)} async-done(((bf16[256,256]{0,1:T(8,128)(2,1)}), bf16[8192,256]{0,1:T(8,128)(2,1)}) %all-gather.9.cloned.1.call-update) | async-done | bytes 4194320 | tf_op jit(solution)/shard_map/all_gather | solution.py:48
  188.6 6.4 %copy.28 = bf16[8192,256]{1,0:T(8,128)(2,1)} copy(bf16[8192,256]{0,1:T(8,128)(2,1)} %all-gather.9.cloned.1.call-done) | data formatting | bytes 8388608 | tf_op jit(solution)/shard_map/reshape | solution.py:48
  195.0 5.0 %gather_fusion = bf16[32,256,256]{2,1,0:T(8,128)(2,1)} fusion(bf16[32,256,256]{2,1,0:T(8,128)(2,1)} %bitcast.59, s32[1024]{0:T(1024)S(1)} %pad_clamp_fusion), kind=kCustom, calls=%fused_computation | custom fusion | bytes 8388736 | tf_op jit(solution)/shard_map/jit(_take)/gather | solution.py:61
  200.0 6.4 %copy.20 = bf16[16,2,256,256]{2,3,1,0:T(8,128)(2,1)} copy(bf16[16,2,256,256]{3,2,1,0:T(8,128)(2,1)} %bitcast.60) | data formatting | bytes 8388608 | tf_op jit(solution)/shard_map/jit(_take)/gather | solution.py:61
  206.4 4.7 %select_select_fusion = bf16[16,2,256,256]{2,3,1,0:T(8,128)(2,1)} fusion(bf16[16,2,256,256]{2,3,1,0:T(8,128)(2,1)} %copy.20, pred[16,2]{1,0:T(8,128)(4,1)S(1)} %copy.18, pred[16,2]{1,0:T(8,128)(4,1)S(1)} %copy.17), kind=kLoop, calls=%fused_computation.6 | loop fusion | flops 4194304 | bytes 8388672 | tf_op jit(solution)/shard_map/jit(_where)/select_n | solution.py:63
  211.1 0.0 copy-start.1
  211.1 7.7 %all-to-all-start = ((bf16[16,2,256,256]{2,3,1,0:T(8,128)(2,1)}), bf16[16,2,256,256]{2,3,1,0:T(8,128)(2,1)}, u32[]{:S(2)}, u32[]{:S(2)}) async-start(bf16[16,2,256,256]{2,3,1,0:T(8,128)(2,1)} %select_select_fusion), calls=%async_computation | async-start | bytes 8388608 | tf_op jit(solution)/shard_map/all_to_all | solution.py:64
  218.9 0.1 constant_dynamic-slice_fusion.1
  219.0 0.6 fusion.44
  222.2 0.1 fusion.16
  222.3 0.0 copy-done.1
  222.3 2.3 collective-permute-start
  224.6 1.4 add_add_fusion
  229.9 92.4 %collective-permute-done = bf16[256,256]{0,1:T(8,128)(2,1)S(1)} collective-permute-done((bf16[256,256]{0,1:T(8,128)(2,1)S(1)}, bf16[256,256]{0,1:T(8,128)(2,1)S(1)}, u32[]{:S(2)}, u32[]{:S(2)}) %collective-permute-start) | collective-permute-done | bytes 131104 | tf_op jit(solution)/shard_map/ppermute | solution.py:12
  322.3 0.0 all-gather.11.cloned.1.call-done
  322.3 3.4 %fusion.9 = bf16[32,4,8,128]{3,2,1,0:T(8,128)(2,1)S(1)} fusion(bf16[256,4096]{1,0:T(8,128)(2,1)S(1)} %copy-done, bf16[4096,512]{1,0:T(8,128)(2,1)} %all-gather.11.cloned.1.call-done), kind=kOutput, calls=%fused_computation.12 | convolution fusion | flops 1073872896 | bytes 6553600 | tf_op jit(solution)/shard_map/dot_general | solution.py:18
  325.8 0.0 all-to-all-done
  325.8 2.7 fusion.42
  328.5 1.2 fusion.2
  329.7 1.3 fusion
  331.0 1.8 fusion.13
  332.8 0.8 copy.24
  (16 shorter events, 0.2 us)
Async XLA Ops:
  6.5 49.5 %copy-start = (bf16[256,4096]{1,0:T(8,128)(2,1)S(1)}, bf16[256,4096]{1,0:T(8,128)(2,1)}, u32[]{:S(2)}) copy-start(bf16[256,4096]{1,0:T(8,128)(2,1)} %param.5) | copy-start | bytes 6291460
  6.5 95.1 %copy-start.2 = (s32[256,2]{0,1:T(2,128)S(1)}, s32[256,2]{0,1:T(2,128)}, u32[]{:S(2)}) copy-start(s32[256,2]{0,1:T(2,128)} %param.9) | copy-start | bytes 6148
  6.5 49.5 %all-gather.7.cloned.1.call-start = ((), (), s32[]{:S(2)}) async-start(), calls=%async_computation.2 | async-start | bytes 1114112 | tf_op jit(solution)/shard_map/all_gather | solution.py:39
  7.3 91.0 %all-gather.5.cloned.1.call-start = ((), (), s32[]{:S(2)}) async-start(), calls=%async_computation.1 | async-start | bytes 1114112 | tf_op jit(solution)/shard_map/all_gather | solution.py:38
  8.0 180.6 %all-gather.9.cloned.1.call-start = ((), (), s32[]{:S(2)}) async-start(), calls=%async_computation.3 | async-start | bytes 4325376 | tf_op jit(solution)/shard_map/all_gather | solution.py:48
  101.0 221.3 %all-gather.11.cloned.1.call-start = ((), (), s32[]{:S(2)}) async-start(), calls=%async_computation.4 | async-start | bytes 4456448 | tf_op jit(solution)/shard_map/all_gather | solution.py:37
  211.1 11.2 %copy-start.1 = (bf16[256,256]{0,1:T(8,128)(2,1)S(1)}, bf16[256,256]{0,1:T(8,128)(2,1)}, u32[]{:S(2)}) copy-start(bf16[256,256]{0,1:T(8,128)(2,1)} %pad_maximum_fusion.2) | copy-start | bytes 393220
  211.1 114.6 %all-to-all-start = ((bf16[16,2,256,256]{2,3,1,0:T(8,128)(2,1)}), bf16[16,2,256,256]{2,3,1,0:T(8,128)(2,1)}, u32[]{:S(2)}, u32[]{:S(2)}) async-start(bf16[16,2,256,256]{2,3,1,0:T(8,128)(2,1)} %select_select_fusion), calls=%async_computation | async-start | bytes 8388608 | tf_op jit(solution)/shard_map/all_to_all | solution.py:64
  222.3 99.9 %collective-permute-start = (bf16[256,256]{0,1:T(8,128)(2,1)S(1)}, bf16[256,256]{0,1:T(8,128)(2,1)S(1)}, u32[]{:S(2)}, u32[]{:S(2)}) collective-permute-start(bf16[256,256]{0,1:T(8,128)(2,1)S(1)} %copy-done.1), channel_id=1, source_target_pairs={{0,1},{1,2},{2,3},{3,4},{4,5},{5,6},{6,7},{7,8},{8,9},{9,10},{10,1... | collective-permute-start | bytes 393224 | tf_op jit(solution)/shard_map/ppermute | solution.py:12
Sparse Core Ops, SparseCore 0:
  9.5 46.5 all-gather.6
  58.2 40.0 all-gather.4
  101.3 87.2 all-gather.8
  190.6 80.9 all-gather.10
where the time goes:
time: 341 us; the launch traced here: 340 us
  waiting for transfers between devices  269 us (79%)
  local copies, waits for them, and re-layouts  22.6 us (7%)
  between operations  19.7 us (6%)
  matrix products  10.5 us (3%)
  starting transfers between devices  10.1 us (3%)
  other arithmetic  8.39 us (2%)
    ppermute x1, waiting for transfers between devices, from_behind(): return lax.ppermute(array, axis, pairs)  92.4 us
    all_gather x1, waiting for transfers between devices, per_device(): lax.all_gather(key_value, 'ctx', axis=0, tiled=True)  86.4 us
    all_gather x1, waiting for transfers between devices, per_device(): lax.all_gather(value_weight, 'fsdp', axis=0, tiled=True)  48 us
    all_gather x1, waiting for transfers between devices, per_device(): lax.all_gather(key_weight, 'fsdp', axis=0, tiled=True)  40.2 us
    gather x2, local copies, waits for them, and re-layouts, per_device(): jnp.take(candidates, (wanted // blocks_group).reshape(-1), axis=0)  11.4 us
    all_to_all x1, starting transfers between devices, per_device(): lax.all_to_all(outgoing, 'fsdp', split_axis=0, concat_axis=0, tiled=True)  7.75 us
    dot_general x3, matrix products, project_rows(): jnp.dot(tokens, weight_piece, preferred_element_type=jnp.float32)  7.53 us
  transfers between devices with their start and end apart: 6, of which 4 were waited for; matrix products, arithmetic and copies ran while one was open for 9% of the time, Pallas kernels for 0%

commit v1 on v0

--- a/solution.py
+++ b/solution.py
@@ -4,6 +4,11 @@
 from jax.sharding import PartitionSpec as P
 
 QH = 4
+
+
+def tiled_gather(x, axis, dim):
+    copies = jnp.concatenate([x] * lax.axis_size(axis), axis=dim)
+    return lax.all_to_all(copies, axis, dim, dim, tiled=True)
 
 
 def from_behind(array, axis, by):
@@ -35,7 +40,7 @@
         tokens,
         (
             lax.all_gather(query_weight, "fsdp", axis=0, tiled=True),
-            lax.all_gather(key_weight, "fsdp", axis=0, tiled=True),
+            tiled_gather(key_weight, "fsdp", 0),
             lax.all_gather(value_weight, "fsdp", axis=0, tiled=True),
         ),
     )

time: 341 us -> 323 us (0.947)
  waiting for transfers between devices: 269 us -> 226 us
  local copies, waits for them, and re-layouts: 22.6 us -> 37.4 us
  starting transfers between devices: 10.1 us -> 20.7 us
    all_gather x1 -> x0, waiting for transfers between devices: 40.2 us -> none  [per_device(): lax.all_gather(key_weight, 'fsdp', axis=0, tiled=True)]
    all_gather x1, waiting for transfers between devices: 48 us -> 20 us  [per_device(): lax.all_gather(value_weight, 'fsdp', axis=0, tiled=True)]
    all_to_all x0 -> x1, waiting for transfers between devices: none -> 26.5 us  [tiled_gather(): return lax.all_to_all(copies, axis, dim, dim, tiled=True)]
    unnamed x6 -> x23, local copies, waits for them, and re-layouts: 0.01 us -> 13.9 us
    all_to_all x0 -> x1, starting transfers between devices: none -> 10.6 us  [tiled_gather(): return lax.all_to_all(copies, axis, dim, dim, tiled=True)]
where the time goes in v1:
time: 323 us; the launch traced here: 322 us
  waiting for transfers between devices  226 us (70%)
  local copies, waits for them, and re-layouts  37.4 us (12%)
  starting transfers between devices  20.7 us (6%)
  between operations  19.8 us (6%)
  matrix products  9.26 us (3%)
  other arithmetic  8.39 us (3%)
    ppermute x1, waiting for transfers between devices, from_behind(): return lax.ppermute(array, axis, pairs)  92.5 us
    all_gather x1, waiting for transfers between devices, per_device(): lax.all_gather(key_value, 'ctx', axis=0, tiled=True)  86 us
    all_to_all x1, waiting for transfers between devices, tiled_gather(): return lax.all_to_all(copies, axis, dim, dim, tiled=True)  26.5 us
    all_gather x1, waiting for transfers between devices, per_device(): lax.all_gather(value_weight, 'fsdp', axis=0, tiled=True)  20 us
    unnamed x23, local copies, waits for them, and re-layouts  13.9 us
    gather x2, local copies, waits for them, and re-layouts, per_device(): jnp.take(candidates, (wanted // blocks_group).reshape(-1), axis=0)  11.4 us
    all_to_all x1, starting transfers between devices, tiled_gather(): return lax.all_to_all(copies, axis, dim, dim, tiled=True)  10.6 us
    all_to_all x1, starting transfers between devices, per_device(): lax.all_to_all(outgoing, 'fsdp', split_axis=0, concat_axis=0, tiled=True)  7.74 us
  transfers between devices with their start and end apart: 6, of which 4 were waited for; matrix products, arithmetic and copies ran while one was open for 9% of the time, Pallas kernels for 0%

profile of v1, /device:TPU:6, one launch (start us, length us, event | category | flops | bytes accessed | tf_op | source)
XLA Modules:
  0.0 321.9 jit_solution(16638646663496316821)
XLA Ops:
  6.5 1.0 constant_dynamic-update-slice_fusion.15
  7.5 0.9 constant_dynamic-update-slice_fusion.14
  8.4 0.9 constant_dynamic-update-slice_fusion.13
  9.2 0.9 constant_dynamic-update-slice_fusion.12
  10.1 0.9 constant_dynamic-update-slice_fusion.11
  10.9 0.9 constant_dynamic-update-slice_fusion.10
  11.8 0.9 constant_dynamic-update-slice_fusion.9
  12.7 0.9 constant_dynamic-update-slice_fusion.8
  13.5 0.9 constant_dynamic-update-slice_fusion.7
  14.4 0.9 constant_dynamic-update-slice_fusion.6
  15.2 0.9 constant_dynamic-update-slice_fusion.5
  16.1 0.9 constant_dynamic-update-slice_fusion.4
  16.9 0.9 constant_dynamic-update-slice_fusion.3
  17.8 0.9 constant_dynamic-update-slice_fusion.2
  18.6 0.9 constant_dynamic-update-slice_fusion.1
  19.5 0.9 constant_dynamic-update-slice_fusion
  20.4 1.0 copy-done.1
  21.3 10.6 %all-to-all-start = ((bf16[16,256,128]{2,1,0:T(8,128)(2,1)}), bf16[16,256,128]{2,1,0:T(8,128)(2,1)S(1)}, u32[]{:S(2)}, u32[]{:S(2)}) async-start(bf16[16,256,128]{2,1,0:T(8,128)(2,1)} %bitcast.66), calls=%async_computation | async-start | bytes 2097152 | tf_op jit(solution)/shard_map/all_to_all | solution.py:11
  31.9 0.7 all-gather.4.cloned.1.call-update
  32.7 26.5 %all-to-all-done = bf16[16,256,128]{2,1,0:T(8,128)(2,1)S(1)} async-done(((bf16[16,256,128]{2,1,0:T(8,128)(2,1)}), bf16[16,256,128]{2,1,0:T(8,128)(2,1)S(1)}, u32[]{:S(2)}, u32[]{:S(2)}) %all-to-all-start) | async-done | bytes 1048608 | tf_op jit(solution)/shard_map/all_to_all | solution.py:11
  59.1 0.8 fusion.10
  60.0 20.0 %all-gather.4.cloned.1.call-done = bf16[4096,128]{1,0:T(8,128)(2,1)} async-done(((bf16[256,128]{1,0:T(8,128)(2,1)}), bf16[4096,128]{1,0:T(8,128)(2,1)}) %all-gather.4.cloned.1.call-update) | async-done | bytes 1048592 | tf_op jit(solution)/shard_map/all_gather | solution.py:44
  80.0 2.0 convolution_convert_fusion.1
  82.1 0.7 pad_maximum_fusion.2
  82.8 0.7 all-gather.8.cloned.1.call-update
  83.5 0.1 constant_dynamic-slice_fusion
  83.6 0.1 copy.15
  83.7 0.1 reshape.213
  83.8 0.1 copy.27
  83.9 0.1 copy.17
  84.0 0.1 copy.18
  84.1 86.0 %all-gather.6.cloned.1.call-done = bf16[8192,256]{0,1:T(8,128)(2,1)} async-done(((bf16[256,256]{0,1:T(8,128)(2,1)}), bf16[8192,256]{0,1:T(8,128)(2,1)}) %all-gather.6.cloned.1.call-update) | async-done | bytes 4194320 | tf_op jit(solution)/shard_map/all_gather | solution.py:53
  170.2 6.4 %copy.28 = bf16[8192,256]{1,0:T(8,128)(2,1)} copy(bf16[8192,256]{0,1:T(8,128)(2,1)} %all-gather.6.cloned.1.call-done) | data formatting | bytes 8388608 | tf_op jit(solution)/shard_map/reshape | solution.py:53
  176.6 5.0 %gather_fusion = bf16[32,256,256]{2,1,0:T(8,128)(2,1)} fusion(bf16[32,256,256]{2,1,0:T(8,128)(2,1)} %bitcast.63, s32[1024]{0:T(1024)S(1)} %pad_clamp_fusion), kind=kCustom, calls=%fused_computation | custom fusion | bytes 8388736 | tf_op jit(solution)/shard_map/jit(_take)/gather | solution.py:66
  181.5 6.4 %copy.20 = bf16[16,2,256,256]{2,3,1,0:T(8,128)(2,1)} copy(bf16[16,2,256,256]{3,2,1,0:T(8,128)(2,1)} %bitcast.64) | data formatting | bytes 8388608 | tf_op jit(solution)/shard_map/jit(_take)/gather | solution.py:66
  187.9 4.7 %select_select_fusion = bf16[16,2,256,256]{2,3,1,0:T(8,128)(2,1)} fusion(bf16[16,2,256,256]{2,3,1,0:T(8,128)(2,1)} %copy.20, pred[16,2]{1,0:T(8,128)(4,1)S(1)} %copy.18, pred[16,2]{1,0:T(8,128)(4,1)S(1)} %copy.17), kind=kLoop, calls=%fused_computation.6 | loop fusion | flops 4194304 | bytes 8388672 | tf_op jit(solution)/shard_map/jit(_where)/select_n | solution.py:68
  192.6 7.7 %all-to-all-start.1 = ((bf16[16,2,256,256]{2,3,1,0:T(8,128)(2,1)}), bf16[16,2,256,256]{2,3,1,0:T(8,128)(2,1)}, u32[]{:S(2)}, u32[]{:S(2)}) async-start(bf16[16,2,256,256]{2,3,1,0:T(8,128)(2,1)} %select_select_fusion), calls=%async_computation.1 | async-start | bytes 8388608 | tf_op jit(solution)/shard_map/all_to_all | solution.py:69
  200.5 0.6 fusion.45
  203.7 0.1 fusion.17
  203.8 2.3 collective-permute-start
  206.1 1.4 add_add_fusion
  211.4 92.5 %collective-permute-done = bf16[256,256]{0,1:T(8,128)(2,1)S(1)} collective-permute-done((bf16[256,256]{0,1:T(8,128)(2,1)S(1)}, bf16[256,256]{0,1:T(8,128)(2,1)S(1)}, u32[]{:S(2)}, u32[]{:S(2)}) %collective-permute-start) | collective-permute-done | bytes 131104 | tf_op jit(solution)/shard_map/ppermute | solution.py:17
  304.0 3.4 %fusion.9 = bf16[32,4,8,128]{3,2,1,0:T(8,128)(2,1)S(1)} fusion(bf16[256,4096]{1,0:T(8,128)(2,1)S(1)} %copy-done, bf16[4096,512]{1,0:T(8,128)(2,1)} %all-gather.8.cloned.1.call-done), kind=kOutput, calls=%fused_computation.12 | convolution fusion | flops 1073872896 | bytes 6553600 | tf_op jit(solution)/shard_map/dot_general | solution.py:23
  307.5 2.7 fusion.43
  310.2 1.2 fusion.2
  311.4 1.3 fusion
  312.7 1.8 fusion.14
  314.5 0.8 copy.24
  (30 shorter events, 0.5 us)
Async XLA Ops:
  6.5 52.6 %copy-start = (bf16[256,4096]{1,0:T(8,128)(2,1)S(1)}, bf16[256,4096]{1,0:T(8,128)(2,1)}, u32[]{:S(2)}) copy-start(bf16[256,4096]{1,0:T(8,128)(2,1)} %param.5) | copy-start | bytes 6291460
  20.3 1.0 copy-start.1
  21.3 62.2 %copy-start.3 = (s32[256,2]{0,1:T(2,128)S(1)}, s32[256,2]{0,1:T(2,128)}, u32[]{:S(2)}) copy-start(s32[256,2]{0,1:T(2,128)} %param.9) | copy-start | bytes 6148
  21.3 37.8 %all-to-all-start = ((bf16[16,256,128]{2,1,0:T(8,128)(2,1)}), bf16[16,256,128]{2,1,0:T(8,128)(2,1)S(1)}, u32[]{:S(2)}, u32[]{:S(2)}) async-start(bf16[16,256,128]{2,1,0:T(8,128)(2,1)} %bitcast.66), calls=%async_computation | async-start | bytes 2097152 | tf_op jit(solution)/shard_map/all_to_all | solution.py:11
  31.9 48.1 %all-gather.4.cloned.1.call-start = ((), (), s32[]{:S(2)}) async-start(), calls=%async_computation.2 | async-start | bytes 1114112 | tf_op jit(solution)/shard_map/all_gather | solution.py:44
  32.6 137.5 %all-gather.6.cloned.1.call-start = ((), (), s32[]{:S(2)}) async-start(), calls=%async_computation.3 | async-start | bytes 4325376 | tf_op jit(solution)/shard_map/all_gather | solution.py:53
  82.7 221.3 %all-gather.8.cloned.1.call-start = ((), (), s32[]{:S(2)}) async-start(), calls=%async_computation.4 | async-start | bytes 4456448 | tf_op jit(solution)/shard_map/all_gather | solution.py:42
  192.6 11.2 %copy-start.2 = (bf16[256,256]{0,1:T(8,128)(2,1)S(1)}, bf16[256,256]{0,1:T(8,128)(2,1)}, u32[]{:S(2)}) copy-start(bf16[256,256]{0,1:T(8,128)(2,1)} %pad_maximum_fusion.2) | copy-start | bytes 393220
  192.6 114.8 %all-to-all-start.1 = ((bf16[16,2,256,256]{2,3,1,0:T(8,128)(2,1)}), bf16[16,2,256,256]{2,3,1,0:T(8,128)(2,1)}, u32[]{:S(2)}, u32[]{:S(2)}) async-start(bf16[16,2,256,256]{2,3,1,0:T(8,128)(2,1)} %select_select_fusion), calls=%async_computation.1 | async-start | bytes 8388608 | tf_op jit(solution)/shard_map/all_to_all | solution.py:69
  203.8 100.1 %collective-permute-start = (bf16[256,256]{0,1:T(8,128)(2,1)S(1)}, bf16[256,256]{0,1:T(8,128)(2,1)S(1)}, u32[]{:S(2)}, u32[]{:S(2)}) collective-permute-start(bf16[256,256]{0,1:T(8,128)(2,1)S(1)} %copy-done.2), channel_id=1, source_target_pairs={{0,1},{1,2},{2,3},{3,4},{4,5},{5,6},{6,7},{7,8},{8,9},{9,10},{10,1... | collective-permute-start | bytes 393224 | tf_op jit(solution)/shard_map/ppermute | solution.py:17
Sparse Core Ops, SparseCore 0:
  34.8 45.1 all-gather.3
  83.0 87.0 all-gather.5
  172.3 80.2 all-gather.7
